TPU v7x, 32 devices: a whole 2x2x4 slice. The times are simulated.
32 devices in a mesh: blk: 8 (over z, y), harvest: 4 (over x, core).
Axes of the slice: x: 2, y: 2, z: 4, core: 2. Of those that a mesh axis runs over, the one named last changes fastest.
Arguments:
- grad_rows: bfloat16 [8192, 8192], P(('blk', 'harvest')), may hold values from -1500 to 1500
- row_weights: float32 [8192], P(('blk', 'harvest')), may hold values from 0.25 to 4
- destinations: int32 [8192, 1], P(('blk', 'harvest')), may hold values from 0 to 7; in each aligned block of 256 rows (0 to 255, 256 to 511, ...) at most 48 rows name the same one
- queries: bfloat16 [128, 8192], P(('blk', 'harvest')), may hold values from -6 to 6
- tile_pattern: int32 [8, 8], replicated, may hold values from 0 to 1, as said below
Outputs:
- scores: bfloat16 [12288, 128], P(('blk', 'harvest'))
Inputs may be any that keep to these rules, and one draw needn't show every extreme that they name: `destinations`: in the rows of one device no owner is named more than 48 times, a bound that some block reaches. tile_pattern[a, b] is 1 where the tile of query block a and owner b is scored.
All inputs are finite; a program needn't handle non-finite values.
Results may differ from a plain program's by a relative error of at most 0.0095.
Values may be sent and summed in bfloat16 or wider, within the bound.
No kernel may reach another device: no remote copies, remote signals or barrier semaphores. Data moves between devices by JAX's collectives and lax.ppermute only.
A program may use at most 128 MiB of HBM per device.

v0:
```python
import math
import jax
import jax.numpy as jnp
from jax import lax
from jax.sharding import PartitionSpec as P


def make_tile(left_rows, weight_scale, shard_rows, tile_mask):
    product = jnp.einsum("sk,pk->sp", left_rows, shard_rows, preferred_element_type=jnp.float32)
    return product * weight_scale[:, None] * tile_mask


def circulate(prepared, folding, initial):
    block_queries = lax.all_gather(prepared, "harvest", axis=0, tiled=True)
    return folding(initial, lax.all_gather(block_queries, "blk", axis=0, tiled=True), jnp.int32(0))


def local(grad_rows, row_weights, destinations, queries, tile_pattern):
    blk_count = lax.axis_size("blk")
    harv_count = lax.axis_size("harvest")
    row_count = grad_rows.shape[0]
    width = grad_rows.shape[1]
    capacity = max(3 * row_count // (2 * blk_count), 2)
    block_size = queries.shape[0] * harv_count
    query_count = block_size * blk_count
    inv_root = 1.0 / math.sqrt(width)
    squares = jnp.sum(row_weights[:, None] * jnp.square(grad_rows.astype(jnp.float32)), axis=0)
    total_sq, total_weight = lax.psum((squares, jnp.sum(row_weights)), ("blk", "harvest"))
    scaling = lax.rsqrt(total_sq / total_weight + 1e-06)
    prepared = (queries.astype(jnp.float32) * scaling).astype(jnp.bfloat16)
    owner_ids = destinations[:, 0]
    one_hot = (owner_ids[:, None] == jnp.arange(blk_count, dtype=jnp.int32)[None, :]).astype(
        jnp.int32
    )
    before = jnp.cumsum(one_hot, axis=0) - one_hot
    slot_rank = jnp.sum(before * one_hot, axis=1)
    slot_index = owner_ids * capacity + slot_rank
    weight_scale = row_weights * inv_root
    slot_total = blk_count * capacity
    bucket_rows = jnp.zeros((slot_total, width), jnp.bfloat16).at[slot_index].set(grad_rows)
    bucket_weights = jnp.zeros((slot_total,), jnp.float32).at[slot_index].set(weight_scale)
    slot_rows, slot_weights = (
        lax.all_to_all(
            bucket_rows.reshape(blk_count, capacity, width),
            "blk",
            split_axis=0,
            concat_axis=0,
            tiled=True,
        ),
        lax.all_to_all(
            bucket_weights.reshape(blk_count, capacity).astype(jnp.bfloat16),
            "blk",
            split_axis=0,
            concat_axis=0,
            tiled=True,
        ).astype(jnp.float32),
    )
    slot_rows = slot_rows.reshape(slot_total, width)
    slot_weights = slot_weights.reshape(slot_total)
    owner_index = lax.axis_index("blk")
    pattern_column = lax.dynamic_slice(tile_pattern, (0, owner_index), (blk_count, 1))[:, 0]
    query_mask = jnp.repeat(pattern_column.astype(jnp.float32), block_size)

    def fold_owner(running, shard_rows, offset):
        tile_mask = query_mask[None, :]
        tile_values = make_tile(slot_rows, slot_weights, shard_rows, tile_mask)
        return lax.dynamic_update_slice_in_dim(running, tile_values, offset, 1)

    initial = jnp.zeros((slot_total, query_count), jnp.float32)
    return circulate(prepared, fold_owner, initial).astype(jnp.bfloat16)


def solution(mesh):
    in_specs = (
        P(("blk", "harvest"), None),
        P(("blk", "harvest")),
        P(("blk", "harvest"), None),
        P(("blk", "harvest"), None),
        P(),
    )
    out_specs = P(("blk", "harvest"), None)
    return jax.shard_map(local, mesh=mesh, in_specs=in_specs, out_specs=out_specs, check_vma=False)
```

profile of v0, /device:TPU:0, one launch (start us, length us, event | category | flops | bytes accessed | tf_op | source)
XLA Modules:
  0.0 264.9 jit_solution(10223305340122949333)
XLA Ops:
  6.5 0.7 fusion.7
  7.2 0.6 reduce-window.6
  7.8 0.2 slice_reduce_fusion
  8.0 0.8 fusion.6
  8.8 0.7 compare_select_fusion
  9.5 1.3 broadcast_multiply_fusion
  10.8 1.4 scatter_custom_fusion.1
  12.2 0.7 convert_element_type.61
  12.9 7.3 %all-to-all-start.1 = ((bf16[8,1,48]{2,1,0:T(2,128)(2,1)}), bf16[8,1,48]{2,1,0:T(2,128)(2,1)S(1)}, u32[]{:S(2)}, u32[]{:S(2)}) async-start(bf16[8,1,48]{2,1,0:T(2,128)(2,1)} %convert_element_type.61), calls=%async_computation.1 | async-start | bytes 8192 | tf_op jit(solution)/shard_map/all_to_all | solution.py:50
  20.2 11.3 %scatter_custom_fusion = bf16[384,8192]{1,0:T(8,128)(2,1)} fusion(s32[256]{0:T(256)S(1)} %bitcast.23, bf16[256,8192]{1,0:T(8,128)(2,1)} %param.5, bf16[]{:T(256)} %constant.10.clone.1), kind=kCustom, calls=%fused_computation.3 | custom fusion | bytes 6291968 | tf_op jit(solution)/shard_map/scatter | solution.py:40
  31.5 6.1 %all-to-all-start = ((bf16[8,48,8192]{2,1,0:T(8,128)(2,1)}), bf16[8,48,8192]{2,1,0:T(8,128)(2,1)}, u32[]{:S(2)}, u32[]{:S(2)}) async-start(bf16[8,48,8192]{2,1,0:T(8,128)(2,1)} %bitcast.18), calls=%async_computation | async-start | bytes 12582912 | tf_op jit(solution)/shard_map/all_to_all | solution.py:43
  37.6 0.0 all-gather.3.cloned.1.call-start
  37.7 3.3 %multiply_reduce_fusion = f32[8192]{0:T(1024)S(1)} fusion(bf16[256,8192]{1,0:T(8,128)(2,1)} %param.5, f32[256]{0:T(256)S(1)} %copy-done.1), kind=kLoop, calls=%fused_computation.2 | loop fusion | flops 8380416 | bytes 4228096 | tf_op jit(solution)/shard_map/reduce_sum | solution.py:27
  41.0 154.6 %all-reduce = (f32[8192]{0:T(1024)S(1)}, f32[]{:T(128)}) all-reduce(f32[8192]{0:T(1024)S(1)} %multiply_reduce_fusion, f32[]{:T(128)} %get-tuple-element.8), channel_id=1, replica_groups=mesh['blk'=8,'harvest'=4] {'blk','harvest'}, use_global_device_ids=true, to_apply=%region_5.6 | all-reduce | flops 8193 | bytes 65544 | tf_op jit(solution)/shard_map/psum | solution.py:28
  195.6 0.7 add_rsqrt_fusion
  196.3 6.5 %all-gather = bf16[4,4,8192]{2,1,0:T(4,128)(2,1)S(1)} all-gather(bf16[1,4,8192]{2,1,0:T(4,128)(2,1)S(1)} %fusion.4), channel_id=1, replica_groups=mesh['blk'=8,'harvest'=4] {'harvest'}, dimensions={0}, use_global_device_ids=true | all-gather | bytes 327680 | tf_op jit(solution)/shard_map/all_gather | solution.py:14
  202.9 0.8 reshape.69
  203.6 0.0 all-gather.3.cloned.1.call-update
  203.7 0.2 convert_reduce_fusion.1
  203.9 0.1 broadcast_in_dim.16
  203.9 0.1 mul.61
  204.1 0.1 reshape.51
  204.1 48.1 %all-gather.3.cloned.1.call-done = bf16[128,8192]{1,0:T(8,128)(2,1)} async-done(((bf16[16,8192]{1,0:T(8,128)(2,1)}), bf16[128,8192]{1,0:T(8,128)(2,1)}) %all-gather.3.cloned.1.call-update) | async-done | bytes 2097168 | tf_op jit(solution)/shard_map/all_gather | solution.py:15
  252.2 5.8 %fusion.3 = bf16[384,128]{1,0:T(8,128)(2,1)} fusion(bf16[384,8192]{1,0:T(8,128)(2,1)} %bitcast.7, bf16[128,8192]{1,0:T(8,128)(2,1)} %all-gather.3.cloned.1.call-done, f32[128]{0:T(128)S(1)} %mul.61, f32[384]{0:T(512)S(1)} %reshape.51), kind=kOutput, calls=%fused_computation.7 | convolution fusion | flops 805453824 | bytes 8488960 | tf_op jit(solution)/shard_map/sk,pk->sp/dot_general | solution.py:9
  (13 shorter events, 0.1 us)
Async XLA Ops:
  12.9 18.5 %all-to-all-start.1 = ((bf16[8,1,48]{2,1,0:T(2,128)(2,1)}), bf16[8,1,48]{2,1,0:T(2,128)(2,1)S(1)}, u32[]{:S(2)}, u32[]{:S(2)}) async-start(bf16[8,1,48]{2,1,0:T(2,128)(2,1)} %convert_element_type.61), calls=%async_computation.1 | async-start | bytes 8192 | tf_op jit(solution)/shard_map/all_to_all | solution.py:50
  31.5 6.2 %copy-start.1 = (f32[256]{0:T(256)S(1)}, f32[256]{0:T(256)}, u32[]{:S(2)}) copy-start(f32[256]{0:T(256)} %param.6) | copy-start | bytes 3076
  31.5 164.8 %copy-start = (bf16[4,8192]{1,0:T(4,128)(2,1)S(1)}, bf16[4,8192]{1,0:T(4,128)(2,1)}, u32[]{:S(2)}) copy-start(bf16[4,8192]{1,0:T(4,128)(2,1)} %param.8) | copy-start | bytes 196612
  31.5 172.2 %copy-start.2 = (s32[8,8]{1,0:T(8,128)S(1)}, s32[8,8]{1,0:T(8,128)}, u32[]{:S(2)}) copy-start(s32[8,8]{1,0:T(8,128)} %param.9) | copy-start | bytes 772
  31.5 220.7 %all-to-all-start = ((bf16[8,48,8192]{2,1,0:T(8,128)(2,1)}), bf16[8,48,8192]{2,1,0:T(8,128)(2,1)}, u32[]{:S(2)}, u32[]{:S(2)}) async-start(bf16[8,48,8192]{2,1,0:T(8,128)(2,1)} %bitcast.18), calls=%async_computation | async-start | bytes 12582912 | tf_op jit(solution)/shard_map/all_to_all | solution.py:43
  37.6 214.6 %all-gather.3.cloned.1.call-start = ((), (), s32[]{:S(2)}) async-start(), calls=%async_computation.2 | async-start | bytes 2359296 | tf_op jit(solution)/shard_map/all_gather | solution.py:15
Sparse Core Ops, SparseCore 0:
  203.8 48.3 all-gather.2
where the time goes:
time: 265 us
  blocking collectives  161 us (61%)
  waiting for transfers between devices  48.1 us (18%)
  local copies, waits for them, and re-layouts  14.6 us (6%)
  starting transfers between devices  13.5 us (5%)
  between operations  13.5 us (5%)
  other arithmetic  8.31 us (3%)
  matrix products  5.85 us (2%)
    psum x1, blocking collectives, local(): lax.psum((squares, jnp.sum(row_weights)), ('blk', 'harvest'))  155 us
    all_gather x1, waiting for transfers between devices, circulate(): lax.all_gather(block_queries, 'blk', axis=0, tiled=True)  48.1 us
    scatter x1, local copies, waits for them, and re-layouts, local(): jnp.zeros((slot_total, width), jnp.bfloat16).at[slot_index].set(grad_rows)  11.3 us
    all_to_all x1, starting transfers between devices, local(): lax.all_to_all(bucket_weights.reshape(blk_count, capacity).astype(jnp.bfl...  7.28 us
    all_gather x1, blocking collectives, circulate(): block_queries = lax.all_gather(prepared, 'harvest', axis=0, tiled=True)  6.53 us
    all_to_all x1, starting transfers between devices, local(): lax.all_to_all(bucket_rows.reshape(blk_count, capacity, width), 'blk', sp...  6.14 us
    dot_general x1, matrix products, make_tile(): jnp.einsum('sk,pk->sp', left_rows, shard_rows, preferred_element_type=jnp...  5.85 us
  transfers between devices with their start and end apart: 3, of which 1 were waited for; matrix products, arithmetic and copies ran while one was open for 6% of the time, Pallas kernels for 0%

commit v1 on v0

--- a/solution.py
+++ b/solution.py
@@ -39,14 +39,30 @@
     slot_total = blk_count * capacity
     bucket_rows = jnp.zeros((slot_total, width), jnp.bfloat16).at[slot_index].set(grad_rows)
     bucket_weights = jnp.zeros((slot_total,), jnp.float32).at[slot_index].set(weight_scale)
+
+    def space_build(shard_in, peer_axis):
+        latest, opened = (lax.axis_size(peer_axis), lax.axis_index(peer_axis))
+        piece_now = shard_in.shape[0] // latest
+        y1 = list(shard_in.shape)
+        y1[0] = piece_now
+        fresh = y1[0]
+        y1[0] = fresh * latest
+        tile_out = jnp.zeros(y1, shard_in.dtype)
+        for rr in range(latest):
+            val2 = lax.dynamic_slice_in_dim(shard_in, (opened ^ rr) * piece_now, piece_now, axis=0)
+            if rr:
+                val2 = lax.ppermute(
+                    val2,
+                    axis_name=peer_axis,
+                    perm=tuple(((nth, nth ^ rr) for nth in range(latest))),
+                )
+            tile_out = lax.dynamic_update_slice_in_dim(
+                tile_out, val2, (opened ^ rr) * fresh, axis=0
+            )
+        return tile_out
+
     slot_rows, slot_weights = (
-        lax.all_to_all(
-            bucket_rows.reshape(blk_count, capacity, width),
-            "blk",
-            split_axis=0,
-            concat_axis=0,
-            tiled=True,
-        ),
+        space_build(bucket_rows.reshape(blk_count, capacity, width), "blk"),
         lax.all_to_all(
             bucket_weights.reshape(blk_count, capacity).astype(jnp.bfloat16),
             "blk",

time: 265 us -> 242 us (0.913)
  the two profiles are of different devices: /device:TPU:0 before, /device:TPU:8 now
where the time goes in v1:
time: 242 us; the launch traced here: 241 us
  blocking collectives  82.3 us (34%)
  waiting for transfers between devices  82.2 us (34%)
  local copies, waits for them, and re-layouts  34.1 us (14%)
  starting transfers between devices  15.7 us (6%)
  between operations  13.5 us (6%)
  other arithmetic  7.59 us (3%)
  matrix products  5.85 us (2%)
    ppermute x7, waiting for transfers between devices, space_build(): lax.ppermute(val2, axis_name=peer_axis, perm=tuple(((nth, nth ^ rr) for n...  82.2 us
    psum x1, blocking collectives, local(): lax.psum((squares, jnp.sum(row_weights)), ('blk', 'harvest'))  75.8 us
    dynamic_update_slice x7, local copies, waits for them, and re-layouts, space_build(): lax.dynamic_update_slice_in_dim(tile_out, val2, (opened ^ rr) * fresh, ax...  12.3 us
    scatter x1, local copies, waits for them, and re-layouts, local(): jnp.zeros((slot_total, width), jnp.bfloat16).at[slot_index].set(grad_rows)  11.3 us
    ppermute x7, starting transfers between devices, space_build(): lax.ppermute(val2, axis_name=peer_axis, perm=tuple(((nth, nth ^ rr) for n...  10.4 us
    all_gather x1, blocking collectives, circulate(): block_queries = lax.all_gather(prepared, 'harvest', axis=0, tiled=True)  6.53 us
    dot_general x1, matrix products, make_tile(): jnp.einsum('sk,pk->sp', left_rows, shard_rows, preferred_element_type=jnp...  5.85 us
    unnamed x11, local copies, waits for them, and re-layouts  5.48 us
  transfers between devices with their start and end apart: 9, of which 2 were waited for; matrix products, arithmetic and copies ran while one was open for 8% of the time, Pallas kernels for 0%

profile of v1, /device:TPU:8, one launch (start us, length us, event | category | flops | bytes accessed | tf_op | source)
XLA Modules:
  0.0 241.3 jit_solution(9055064896864787328)
XLA Ops:
  9.5 11.3 %scatter_custom_fusion = bf16[384,8192]{1,0:T(8,128)(2,1)} fusion(s32[256]{0:T(256)S(1)} %bitcast.23, bf16[256,8192]{1,0:T(8,128)(2,1)} %param.5, bf16[]{:T(256)} %constant.17.clone.1), kind=kCustom, calls=%fused_computation.3 | custom fusion | bytes 6291968 | tf_op jit(solution)/shard_map/scatter | solution.py:40
  21.5 2.0 copy-done
  23.6 1.7 constant_dynamic-slice_fusion.1
  25.3 2.7 %copy-done.1 = bf16[8,48,8192]{2,1,0:T(8,128)(2,1)} copy-done((bf16[8,48,8192]{2,1,0:T(8,128)(2,1)}, bf16[8,48,8192]{2,1,0:T(8,128)(2,1)S(1)}, u32[]{:S(2)}) %copy-start.1) | copy-done | bytes 6291480
  28.0 1.5 collective-permute-start
  29.9 1.5 collective-permute-start.2
  31.4 2.6 %collective-permute-start.3 = (bf16[1,48,8192]{2,1,0:T(8,128)(2,1)S(1)}, bf16[1,48,8192]{2,1,0:T(8,128)(2,1)}, u32[]{:S(2)}, u32[]{:S(2)}) collective-permute-start(bf16[1,48,8192]{2,1,0:T(8,128)(2,1)S(1)} %get-tuple-element.10), channel_id=1, source_target_pairs={{0,16},{4,20},{8,24},{12,28},{16,0},{20,4},{24,8},{28,12},{1,17},{... | collective-permute-start | bytes 2359304 | tf_op jit(solution)/shard_map/ppermute | solution.py:54
  34.0 1.3 collective-permute-start.4
  35.9 1.4 scatter_custom_fusion.1
  38.0 5.3 %all-to-all-start = ((bf16[8,1,48]{2,1,0:T(2,128)(2,1)}), bf16[8,1,48]{2,1,0:T(2,128)(2,1)S(1)}, u32[]{:S(2)}, u32[]{:S(2)}) async-start(bf16[8,1,48]{2,1,0:T(2,128)(2,1)} %convert_element_type.61), calls=%async_computation | async-start | bytes 8192 | tf_op jit(solution)/shard_map/all_to_all | solution.py:66
  43.4 3.3 %multiply_reduce_fusion = f32[8192]{0:T(1024)S(1)} fusion(bf16[256,8192]{1,0:T(8,128)(2,1)} %param.5, f32[256]{0:T(256)S(1)} %copy-done.3), kind=kLoop, calls=%fused_computation.2 | loop fusion | flops 8380416 | bytes 4228096 | tf_op jit(solution)/shard_map/reduce_sum | solution.py:27
  46.7 75.8 %all-reduce = (f32[8192]{0:T(1024)S(1)}, f32[]{:T(128)}) all-reduce(f32[8192]{0:T(1024)S(1)} %multiply_reduce_fusion, f32[]{:T(128)} %get-tuple-element.16), channel_id=1, replica_groups=mesh['blk'=8,'harvest'=4] {'blk','harvest'}, use_global_device_ids=true, to_apply=%region_5.6 | all-reduce | flops 8193 | bytes 65544 | tf_op jit(solution)/shard_map/psum | solution.py:28
  123.2 6.5 %all-gather = bf16[4,4,8192]{2,1,0:T(4,128)(2,1)S(1)} all-gather(bf16[1,4,8192]{2,1,0:T(4,128)(2,1)S(1)} %fusion.4), channel_id=1, replica_groups=mesh['blk'=8,'harvest'=4] {'harvest'}, dimensions={0}, use_global_device_ids=true | all-gather | bytes 327680 | tf_op jit(solution)/shard_map/all_gather | solution.py:14
  131.7 2.1 constant_dynamic-update-slice_fusion.6
  133.7 2.4 collective-permute-start.6
  136.1 2.1 constant_dynamic-update-slice_fusion.5
  138.2 2.1 constant_dynamic-update-slice_fusion.4
  140.3 2.1 constant_dynamic-update-slice_fusion.3
  142.4 2.1 constant_dynamic-update-slice_fusion.2
  144.5 57.1 %collective-permute-done.5 = bf16[1,48,8192]{2,1,0:T(8,128)(2,1)S(1)} collective-permute-done((bf16[1,48,8192]{2,1,0:T(8,128)(2,1)S(1)}, bf16[1,48,8192]{2,1,0:T(8,128)(2,1)S(1)}, u32[]{:S(2)}, u32[]{:S(2)}) %collective-permute-start.5) | collective-permute-done | bytes 786464 | tf_op jit(solution)/shard_map/ppermute | solution.py:54
  201.6 0.9 constant_dynamic-update-slice_fusion.1
  202.5 25.1 %collective-permute-done.6 = bf16[1,48,8192]{2,1,0:T(8,128)(2,1)S(1)} collective-permute-done((bf16[1,48,8192]{2,1,0:T(8,128)(2,1)S(1)}, bf16[1,48,8192]{2,1,0:T(8,128)(2,1)S(1)}, u32[]{:S(2)}, u32[]{:S(2)}) %collective-permute-start.6) | collective-permute-done | bytes 786464 | tf_op jit(solution)/shard_map/ppermute | solution.py:54
  227.7 0.9 constant_dynamic-update-slice_fusion
  228.6 5.8 %fusion.3 = bf16[384,128]{1,0:T(8,128)(2,1)} fusion(bf16[384,8192]{1,0:T(8,128)(2,1)} %bitcast.19, bf16[128,8192]{1,0:T(8,128)(2,1)} %all-gather.3.cloned.1.call-done, f32[128]{0:T(128)S(1)} %mul.61, f32[384]{0:T(512)S(1)} %reshape.51), kind=kOutput, calls=%fused_computation.7 | convolution fusion | flops 805453824 | bytes 8488960 | tf_op jit(solution)/shard_map/sk,pk->sp/dot_general | solution.py:9
  (38 shorter events, 8.0 us)
Async XLA Ops:
  20.8 2.8 %copy-start = (bf16[384,8192]{1,0:T(8,128)(2,1)S(1)}, bf16[384,8192]{1,0:T(8,128)(2,1)}, u32[]{:S(2)}) copy-start(bf16[384,8192]{1,0:T(8,128)(2,1)} %scatter_custom_fusion) | copy-start | bytes 18874372
  23.6 11.8 %copy-start.3 = (f32[256]{0:T(256)S(1)}, f32[256]{0:T(256)}, u32[]{:S(2)}) copy-start(f32[256]{0:T(256)} %param.6) | copy-start | bytes 3076
  23.6 99.6 %copy-start.2 = (bf16[4,8192]{1,0:T(4,128)(2,1)S(1)}, bf16[4,8192]{1,0:T(4,128)(2,1)}, u32[]{:S(2)}) copy-start(bf16[4,8192]{1,0:T(4,128)(2,1)} %param.8) | copy-start | bytes 196612
  23.6 107.0 %copy-start.4 = (s32[8,8]{1,0:T(8,128)S(1)}, s32[8,8]{1,0:T(8,128)}, u32[]{:S(2)}) copy-start(s32[8,8]{1,0:T(8,128)} %param.9) | copy-start | bytes 772
  25.3 2.7 %copy-start.1 = (bf16[8,48,8192]{2,1,0:T(8,128)(2,1)}, bf16[8,48,8192]{2,1,0:T(8,128)(2,1)S(1)}, u32[]{:S(2)}) copy-start(bf16[8,48,8192]{2,1,0:T(8,128)(2,1)S(1)} %get-tuple-element.14) | copy-start | bytes 18874372
  28.0 103.0 %collective-permute-start = (bf16[1,48,8192]{2,1,0:T(8,128)(2,1)}, bf16[1,48,8192]{2,1,0:T(8,128)(2,1)}, u32[]{:S(2)}, u32[]{:S(2)}) collective-permute-start(bf16[1,48,8192]{2,1,0:T(8,128)(2,1)} %get-tuple-element.13), channel_id=1, source_target_pairs={{0,4},{4,0},{8,12},{12,8},{16,20},{20,16},{24,28},{28,24},{1,5},{5... | collective-permute-start | bytes 2359304 | tf_op jit(solution)/shard_map/ppermute | solution.py:54
  29.5 104.3 %collective-permute-start.1 = (bf16[1,48,8192]{2,1,0:T(8,128)(2,1)}, bf16[1,48,8192]{2,1,0:T(8,128)(2,1)}, u32[]{:S(2)}, u32[]{:S(2)}) collective-permute-start(bf16[1,48,8192]{2,1,0:T(8,128)(2,1)} %get-tuple-element.12), channel_id=1, source_target_pairs={{0,8},{4,12},{8,0},{12,4},{16,24},{20,28},{24,16},{28,20},{1,9},{5... | collective-permute-start | bytes 2359304 | tf_op jit(solution)/shard_map/ppermute | solution.py:54
  29.9 108.3 %collective-permute-start.2 = (bf16[1,48,8192]{2,1,0:T(8,128)(2,1)}, bf16[1,48,8192]{2,1,0:T(8,128)(2,1)}, u32[]{:S(2)}, u32[]{:S(2)}) collective-permute-start(bf16[1,48,8192]{2,1,0:T(8,128)(2,1)} %get-tuple-element.11), channel_id=1, source_target_pairs={{0,12},{4,8},{8,4},{12,0},{16,28},{20,24},{24,20},{28,16},{1,13},{... | collective-permute-start | bytes 2359304 | tf_op jit(solution)/shard_map/ppermute | solution.py:54
  31.4 108.9 %collective-permute-start.3 = (bf16[1,48,8192]{2,1,0:T(8,128)(2,1)S(1)}, bf16[1,48,8192]{2,1,0:T(8,128)(2,1)}, u32[]{:S(2)}, u32[]{:S(2)}) collective-permute-start(bf16[1,48,8192]{2,1,0:T(8,128)(2,1)S(1)} %get-tuple-element.10), channel_id=1, source_target_pairs={{0,16},{4,20},{8,24},{12,28},{16,0},{20,4},{24,8},{28,12},{1,17},{... | collective-permute-start | bytes 2359304 | tf_op jit(solution)/shard_map/ppermute | solution.py:54
  34.0 108.4 %collective-permute-start.4 = (bf16[1,48,8192]{2,1,0:T(8,128)(2,1)S(1)}, bf16[1,48,8192]{2,1,0:T(8,128)(2,1)}, u32[]{:S(2)}, u32[]{:S(2)}) collective-permute-start(bf16[1,48,8192]{2,1,0:T(8,128)(2,1)S(1)} %get-tuple-element.9), channel_id=1, source_target_pairs={{0,20},{4,16},{8,28},{12,24},{16,4},{20,0},{24,12},{28,8},{1,21},{... | collective-permute-start | bytes 2359304 | tf_op jit(solution)/shard_map/ppermute | solution.py:54
  38.0 92.9 %all-to-all-start = ((bf16[8,1,48]{2,1,0:T(2,128)(2,1)}), bf16[8,1,48]{2,1,0:T(2,128)(2,1)S(1)}, u32[]{:S(2)}, u32[]{:S(2)}) async-start(bf16[8,1,48]{2,1,0:T(2,128)(2,1)} %convert_element_type.61), calls=%async_computation | async-start | bytes 8192 | tf_op jit(solution)/shard_map/all_to_all | solution.py:66
  43.4 185.2 %all-gather.3.cloned.1.call-start = ((), (), s32[]{:S(2)}) async-start(), calls=%async_computation.1 | async-start | bytes 2359296 | tf_op jit(solution)/shard_map/all_gather | solution.py:15
  131.0 70.6 %collective-permute-start.5 = (bf16[1,48,8192]{2,1,0:T(8,128)(2,1)S(1)}, bf16[1,48,8192]{2,1,0:T(8,128)(2,1)S(1)}, u32[]{:S(2)}, u32[]{:S(2)}) collective-permute-start(bf16[1,48,8192]{2,1,0:T(8,128)(2,1)S(1)} %get-tuple-element.8), channel_id=1, source_target_pairs={{0,24},{4,28},{8,16},{12,20},{16,8},{20,12},{24,0},{28,4},{1,25},{... | collective-permute-start | bytes 2359304 | tf_op jit(solution)/shard_map/ppermute | solution.py:54
  133.7 93.9 %collective-permute-start.6 = (bf16[1,48,8192]{2,1,0:T(8,128)(2,1)S(1)}, bf16[1,48,8192]{2,1,0:T(8,128)(2,1)S(1)}, u32[]{:S(2)}, u32[]{:S(2)}) collective-permute-start(bf16[1,48,8192]{2,1,0:T(8,128)(2,1)S(1)} %get-tuple-element.7), channel_id=1, source_target_pairs={{0,28},{4,24},{8,20},{12,16},{16,12},{20,8},{24,4},{28,0},{1,29},{... | collective-permute-start | bytes 2359304 | tf_op jit(solution)/shard_map/ppermute | solution.py:54
Sparse Core Ops, SparseCore 0:
  130.7 83.0 all-gather.2
